TPU v7x, 512 devices: a whole 4x8x8 slice. The times are simulated.
512 devices in a mesh: grid: 64 (over x, z, core), orb: 8 (over y).
Axes of the slice: x: 4, y: 8, z: 8, core: 2. Of those that a mesh axis runs over, the one named last changes fastest.
Arguments:
- orbitals: float32 [256, 16, 16, 1024], P('grid', None, None, 'orb'), may hold values from -15 to 15
- potential: float32 [256, 16, 16], P('grid'), may hold values from -2 to 0
Outputs:
- filtered: float32 [256, 16, 16, 1024], P('grid', None, None, 'orb')
- hamiltonian_block: float32 [1024, 1024], P('orb', 'grid')
- margin_block: float32 [1024, 1024], P('orb', 'grid')
All inputs are finite; a program needn't handle non-finite values.
Results may differ from a plain program's by a relative error of at most 0.0039.
Values may be sent and summed in bfloat16 or wider, within the bound.
No kernel may reach another device: no remote copies, remote signals or barrier semaphores. Data moves between devices by JAX's collectives and lax.ppermute only.
A program may use at most 64 MiB of HBM per device.

v0:
```python
import jax
import jax.numpy as jnp
from jax import lax
from jax.sharding import PartitionSpec as P

DEGREE = 4
STENCIL = (-205.0 / 72.0, 8.0 / 5.0, -1.0 / 5.0, 8.0 / 315.0, -1.0 / 560.0)
LOWER_EDGE = -2.0
CUT_EDGE = 1.5
UPPER_EDGE = 10.0
EPSILON = 1e-06


def halo_layers(shard, width):
    size = lax.axis_size("grid")
    length = shard.shape[0]
    up = [(i, i + 1) for i in range(size - 1)]
    down = [(j, i) for i, j in up]
    last = lax.slice_in_dim(shard, length - width, length, axis=0).astype(jnp.bfloat16)
    initial = lax.slice_in_dim(shard, 0, width, axis=0).astype(jnp.bfloat16)
    before = lax.ppermute(last, "grid", up).astype(shard.dtype)
    after = lax.ppermute(initial, "grid", down).astype(shard.dtype)
    return jnp.concatenate([before, shard, after], axis=0)


def plane_matrix(rows_y, cols_x):
    flat_count = rows_y * cols_x
    index_all = jnp.arange(flat_count, dtype=jnp.int32)
    row_y = (index_all // cols_x)[:, None]
    row_x = (index_all % cols_x)[:, None]
    col_y = (index_all // cols_x)[None, :]
    col_x = (index_all % cols_x)[None, :]
    delta_y = jnp.mod(row_y - col_y, rows_y)
    delta_x = jnp.mod(row_x - col_x, cols_x)
    same_y = delta_y == 0
    same_x = delta_x == 0
    matrix = jnp.zeros((flat_count, flat_count), jnp.float32)
    for offset in range(1, 5):
        for signed in (offset, -offset):
            hit_y = jnp.logical_and(same_x, delta_y == signed % rows_y)
            hit_x = jnp.logical_and(same_y, delta_x == signed % cols_x)
            matrix = matrix + STENCIL[offset] * (
                hit_y.astype(jnp.float32) + hit_x.astype(jnp.float32)
            )
    return matrix


def apply_hamiltonian(current, potential, plane):
    layers, rows_y, cols_x, width = current.shape
    padded = halo_layers(current, 4)
    laplacian = 3.0 * STENCIL[0] * current
    for offset in range(1, 5):
        laplacian = laplacian + STENCIL[offset] * (
            padded[4 + offset : 4 + offset + layers] + padded[4 - offset : 4 - offset + layers]
        )
    flat = current.reshape(layers, rows_y * cols_x, width)
    in_plane = jnp.einsum(
        "pq,zqo->zpo",
        plane,
        flat,
        precision=lax.Precision.HIGHEST,
        preferred_element_type=jnp.float32,
    )
    laplacian = laplacian + in_plane.reshape(current.shape)
    return -0.5 * laplacian + potential[:, :, :, None] * current


def chebyshev(initial, potential, plane):
    half_width = (UPPER_EDGE - CUT_EDGE) / 2.0
    centre = (UPPER_EDGE + CUT_EDGE) / 2.0
    sigma_now = half_width / (LOWER_EDGE - centre)
    gamma_ratio = 2.0 / sigma_now
    previous = initial
    current = (
        sigma_now / half_width * (apply_hamiltonian(previous, potential, plane) - centre * previous)
    )
    for degree_step in range(DEGREE - 1):
        sigma_next = 1.0 / (gamma_ratio - sigma_now)
        following = (
            2.0
            * sigma_next
            / half_width
            * (apply_hamiltonian(current, potential, plane) - centre * current)
            - sigma_now * sigma_next * previous
        )
        previous, current, sigma_now = (current, following, sigma_next)
    return current


def contract_points(left_side, right_side):
    return lax.dot_general(
        left_side, right_side, (((0,), (0,)), ((), ())), preferred_element_type=jnp.float32
    )


def reduce_scatter_grid(slots):
    size = slots.shape[0]
    bits = size.bit_length() - 1
    me = lax.axis_index("grid")
    rest = slots.shape[1:]
    buf = slots.reshape((2,) * bits + rest)
    for bit in range(bits):
        axis = bits - 1 - bit
        mine = me >> bit & 1
        low = lax.index_in_dim(buf, 0, axis=axis, keepdims=False)
        high = lax.index_in_dim(buf, 1, axis=axis, keepdims=False)
        keep = jnp.where(mine == 1, high, low)
        send = jnp.where(mine == 1, low, high)
        pairs = [(i, i ^ 1 << bit) for i in range(size)]
        buf = keep + lax.ppermute(send, "grid", pairs)
    return buf


def on_device(orbitals, potential):
    own_width = orbitals.shape[3]
    point_count = orbitals.shape[0] * orbitals.shape[1] * orbitals.shape[2]
    grid_size = lax.axis_size("grid")
    point_total = float(point_count * grid_size)
    plane = plane_matrix(orbitals.shape[1], orbitals.shape[2])
    result_block = chebyshev(orbitals, potential, plane)
    own_squares = jnp.sum(result_block * result_block, axis=(0, 1, 2))
    rounded_orbitals = result_block.astype(jnp.bfloat16).reshape(point_count, own_width)
    rounded_image = (
        apply_hamiltonian(result_block, potential, plane)
        .astype(jnp.bfloat16)
        .reshape(point_count, own_width)
    )
    orbitals_all = lax.all_gather(rounded_orbitals, "orb", axis=1, tiled=True)
    total_width = orbitals_all.shape[1]
    rows = total_width // grid_size
    hamiltonian_part = contract_points(orbitals_all, rounded_image)
    margin_part = contract_points(orbitals_all, rounded_orbitals)
    wide = orbitals_all.astype(jnp.float32)
    column_squares = jnp.sum(wide * wide, axis=0)
    body = jnp.concatenate(
        [
            hamiltonian_part.reshape(grid_size, rows, own_width),
            margin_part.reshape(grid_size, rows, own_width),
        ],
        axis=2,
    )
    tail = jnp.concatenate(
        [
            column_squares.reshape(grid_size, rows),
            jnp.broadcast_to(own_squares[None, :], (grid_size, own_width)),
            jnp.zeros((grid_size, own_width - rows), jnp.float32),
        ],
        axis=1,
    )
    slots = jnp.concatenate([body, tail[:, None, :]], axis=1)
    combined = reduce_scatter_grid(slots)
    scale_own = 1.0 / jnp.sqrt(combined[rows, rows : rows + own_width] / point_total + EPSILON)
    column_scale = 1.0 / jnp.sqrt(combined[rows, :rows] / point_total + EPSILON)
    filtered = result_block * scale_own
    pair_scale = scale_own[:, None] * column_scale[None, :] / point_total
    hamiltonian_block = combined[:rows, :own_width].T * pair_scale
    margin_block = combined[:rows, own_width:].T * pair_scale
    return (filtered, hamiltonian_block, margin_block)


def solution(mesh):
    placed = (P("grid", None, None, "orb"), P("grid", None, None))
    return jax.shard_map(
        on_device,
        mesh=mesh,
        in_specs=placed,
        out_specs=(P("grid", None, None, "orb"), P("orb", "grid"), P("orb", "grid")),
        check_vma=False,
    )
```

profile of v0, /device:TPU:2, one launch (start us, length us, event | category | flops | bytes accessed | tf_op | source)
XLA Modules:
  0.0 181.1 jit_solution(14058231074587495252)
XLA Ops:
  8.3 10.4 %collective-permute-start = (bf16[4,16,16,128]{3,2,1,0:T(8,128)(2,1)S(1)}, bf16[4,16,16,128]{3,2,1,0:T(8,128)(2,1)S(1)}, u32[]{:S(2)}, u32[]{:S(2)}) collective-permute-start(bf16[4,16,16,128]{3,2,1,0:T(8,128)(2,1)S(1)} %convert_element_type.233), channel_id=1, source_target_pairs={{8,0},{16,8},{24,16},{32,24},{40,32},{48,40},{56,48},{64,56},{72,6... | collective-permute-start | bytes 786440 | tf_op jit(solution)/shard_map/ppermute | solution.py:22
  18.7 1.9 %collective-permute-start.1 = (bf16[4,16,16,128]{3,2,1,0:T(8,128)(2,1)S(1)}, bf16[4,16,16,128]{3,2,1,0:T(8,128)(2,1)S(1)}, u32[]{:S(2)}, u32[]{:S(2)}) collective-permute-start(bf16[4,16,16,128]{3,2,1,0:T(8,128)(2,1)S(1)} %convert_element_type.233), channel_id=1, source_target_pairs={{0,8},{8,16},{16,24},{24,32},{32,40},{40,48},{48,56},{56,64},{64,7... | collective-permute-start | bytes 786440 | tf_op jit(solution)/shard_map/ppermute | solution.py:21
  21.4 2.7 %fusion.102 = f32[256,4,128]{2,0,1:T(8,128)S(1)} fusion(f32[4,256,128]{2,1,0:T(8,128)} %bitcast.96, s32[256]{0:T(256)S(1)} %get-tuple-element.22, s32[256]{0:T(256)S(1)} %get-tuple-element.23), kind=kOutput, calls=%fused_computation.176 | convolution fusion | flops 408944640 | bytes 1050624 | tf_op jit(solution)/shard_map/pq,zqo->zpo/dot_general | solution.py:57
  24.2 4.3 %collective-permute-done.1 = bf16[4,16,16,128]{3,2,1,0:T(8,128)(2,1)S(1)} collective-permute-done((bf16[4,16,16,128]{3,2,1,0:T(8,128)(2,1)S(1)}, bf16[4,16,16,128]{3,2,1,0:T(8,128)(2,1)S(1)}, u32[]{:S(2)}, u32[]{:S(2)}) %collective-permute-start.1) | collective-permute-done | bytes 262176 | tf_op jit(solution)/shard_map/ppermute | solution.py:21
  28.9 1.9 %collective-permute-start.2 = (bf16[4,16,16,128]{3,2,1,0:T(8,128)(2,1)S(1)}, bf16[4,16,16,128]{3,2,1,0:T(8,128)(2,1)S(1)}, u32[]{:S(2)}, u32[]{:S(2)}) collective-permute-start(bf16[4,16,16,128]{3,2,1,0:T(8,128)(2,1)S(1)} %get-tuple-element.9), channel_id=1, source_target_pairs={{8,0},{16,8},{24,16},{32,24},{40,32},{48,40},{56,48},{64,56},{72,6... | collective-permute-start | bytes 786440 | tf_op jit(solution)/shard_map/ppermute | solution.py:22
  30.8 2.4 %collective-permute-start.3 = (bf16[4,16,16,128]{3,2,1,0:T(8,128)(2,1)S(1)}, bf16[4,16,16,128]{3,2,1,0:T(8,128)(2,1)S(1)}, u32[]{:S(2)}, u32[]{:S(2)}) collective-permute-start(bf16[4,16,16,128]{3,2,1,0:T(8,128)(2,1)S(1)} %get-tuple-element.9), channel_id=1, source_target_pairs={{0,8},{8,16},{16,24},{24,32},{32,40},{40,48},{48,56},{56,64},{64,7... | collective-permute-start | bytes 786440 | tf_op jit(solution)/shard_map/ppermute | solution.py:21
  33.3 1.9 %convolution_bitcast_fusion.3 = f32[4,256,128]{1,2,0:T(8,128)S(1)} fusion(f32[4,256,128]{2,1,0:T(8,128)S(1)} %bitcast.101, s32[256]{0:T(256)S(1)} %get-tuple-element.22, s32[256]{0:T(256)S(1)} %get-tuple-element.23), kind=kOutput, calls=%fused_computation.44 | convolution fusion | flops 408944640 | bytes 1050624 | tf_op jit(solution)/shard_map/pq,zqo->zpo/dot_general | solution.py:57
  35.5 5.1 %collective-permute-done.3 = bf16[4,16,16,128]{3,2,1,0:T(8,128)(2,1)S(1)} collective-permute-done((bf16[4,16,16,128]{3,2,1,0:T(8,128)(2,1)S(1)}, bf16[4,16,16,128]{3,2,1,0:T(8,128)(2,1)S(1)}, u32[]{:S(2)}, u32[]{:S(2)}) %collective-permute-start.3) | collective-permute-done | bytes 262176 | tf_op jit(solution)/shard_map/ppermute | solution.py:21
  41.1 1.9 %collective-permute-start.4 = (bf16[4,16,16,128]{3,2,1,0:T(8,128)(2,1)S(1)}, bf16[4,16,16,128]{3,2,1,0:T(8,128)(2,1)S(1)}, u32[]{:S(2)}, u32[]{:S(2)}) collective-permute-start(bf16[4,16,16,128]{3,2,1,0:T(8,128)(2,1)S(1)} %get-tuple-element.7), channel_id=1, source_target_pairs={{8,0},{16,8},{24,16},{32,24},{40,32},{48,40},{56,48},{64,56},{72,6... | collective-permute-start | bytes 786440 | tf_op jit(solution)/shard_map/ppermute | solution.py:22
  43.1 2.4 %collective-permute-start.5 = (bf16[4,16,16,128]{3,2,1,0:T(8,128)(2,1)S(1)}, bf16[4,16,16,128]{3,2,1,0:T(8,128)(2,1)S(1)}, u32[]{:S(2)}, u32[]{:S(2)}) collective-permute-start(bf16[4,16,16,128]{3,2,1,0:T(8,128)(2,1)S(1)} %get-tuple-element.7), channel_id=1, source_target_pairs={{0,8},{8,16},{16,24},{24,32},{32,40},{40,48},{48,56},{56,64},{64,7... | collective-permute-start | bytes 786440 | tf_op jit(solution)/shard_map/ppermute | solution.py:21
  45.5 1.9 %convolution_bitcast_fusion.2 = f32[4,256,128]{1,2,0:T(8,128)S(1)} fusion(f32[4,256,128]{2,1,0:T(8,128)S(1)} %bitcast.97, s32[256]{0:T(256)S(1)} %get-tuple-element.22, s32[256]{0:T(256)S(1)} %get-tuple-element.23), kind=kOutput, calls=%fused_computation.43 | convolution fusion | flops 408944640 | bytes 1050624 | tf_op jit(solution)/shard_map/pq,zqo->zpo/dot_general | solution.py:57
  47.7 5.2 %collective-permute-done.5 = bf16[4,16,16,128]{3,2,1,0:T(8,128)(2,1)S(1)} collective-permute-done((bf16[4,16,16,128]{3,2,1,0:T(8,128)(2,1)S(1)}, bf16[4,16,16,128]{3,2,1,0:T(8,128)(2,1)S(1)}, u32[]{:S(2)}, u32[]{:S(2)}) %collective-permute-start.5) | collective-permute-done | bytes 262176 | tf_op jit(solution)/shard_map/ppermute | solution.py:21
  53.3 1.9 %collective-permute-start.6 = (bf16[4,16,16,128]{3,2,1,0:T(8,128)(2,1)S(1)}, bf16[4,16,16,128]{3,2,1,0:T(8,128)(2,1)S(1)}, u32[]{:S(2)}, u32[]{:S(2)}) collective-permute-start(bf16[4,16,16,128]{3,2,1,0:T(8,128)(2,1)S(1)} %get-tuple-element.5), channel_id=1, source_target_pairs={{8,0},{16,8},{24,16},{32,24},{40,32},{48,40},{56,48},{64,56},{72,6... | collective-permute-start | bytes 786440 | tf_op jit(solution)/shard_map/ppermute | solution.py:22
  55.2 2.4 %collective-permute-start.7 = (bf16[4,16,16,128]{3,2,1,0:T(8,128)(2,1)S(1)}, bf16[4,16,16,128]{3,2,1,0:T(8,128)(2,1)S(1)}, u32[]{:S(2)}, u32[]{:S(2)}) collective-permute-start(bf16[4,16,16,128]{3,2,1,0:T(8,128)(2,1)S(1)} %get-tuple-element.5), channel_id=1, source_target_pairs={{0,8},{8,16},{16,24},{24,32},{32,40},{40,48},{48,56},{56,64},{64,7... | collective-permute-start | bytes 786440 | tf_op jit(solution)/shard_map/ppermute | solution.py:21
  57.7 1.9 %convolution_bitcast_fusion.1 = f32[4,256,128]{1,2,0:T(8,128)S(1)} fusion(f32[4,256,128]{2,1,0:T(8,128)S(1)} %bitcast.106, s32[256]{0:T(256)S(1)} %get-tuple-element.22, s32[256]{0:T(256)S(1)} %get-tuple-element.23), kind=kOutput, calls=%fused_computation.42 | convolution fusion | flops 408944640 | bytes 1050624 | tf_op jit(solution)/shard_map/pq,zqo->zpo/dot_general | solution.py:57
  59.8 5.2 %collective-permute-done.7 = bf16[4,16,16,128]{3,2,1,0:T(8,128)(2,1)S(1)} collective-permute-done((bf16[4,16,16,128]{3,2,1,0:T(8,128)(2,1)S(1)}, bf16[4,16,16,128]{3,2,1,0:T(8,128)(2,1)S(1)}, u32[]{:S(2)}, u32[]{:S(2)}) %collective-permute-start.7) | collective-permute-done | bytes 262176 | tf_op jit(solution)/shard_map/ppermute | solution.py:21
  66.4 1.9 %collective-permute-start.9 = (bf16[4,16,16,128]{3,2,1,0:T(8,128)(2,1)}, bf16[4,16,16,128]{3,2,1,0:T(8,128)(2,1)S(1)}, u32[]{:S(2)}, u32[]{:S(2)}) collective-permute-start(bf16[4,16,16,128]{3,2,1,0:T(8,128)(2,1)} %convert_element_type.261), channel_id=1, source_target_pairs={{0,8},{8,16},{16,24},{24,32},{32,40},{40,48},{48,56},{56,64},{64,7... | collective-permute-start | bytes 786440 | tf_op jit(solution)/shard_map/ppermute | solution.py:21
  68.3 5.9 %collective-permute-start.8 = (bf16[4,16,16,128]{3,2,1,0:T(8,128)(2,1)}, bf16[4,16,16,128]{3,2,1,0:T(8,128)(2,1)S(1)}, u32[]{:S(2)}, u32[]{:S(2)}) collective-permute-start(bf16[4,16,16,128]{3,2,1,0:T(8,128)(2,1)} %convert_element_type.261), channel_id=1, source_target_pairs={{8,0},{16,8},{24,16},{32,24},{40,32},{48,40},{56,48},{64,56},{72,6... | collective-permute-start | bytes 786440 | tf_op jit(solution)/shard_map/ppermute | solution.py:22
  74.3 1.9 %convolution_bitcast_fusion = f32[4,256,128]{1,2,0:T(8,128)S(1)} fusion(f32[4,256,128]{2,1,0:T(8,128)S(1)} %bitcast.95, s32[256]{0:T(256)S(1)} %get-tuple-element.22, s32[256]{0:T(256)S(1)} %get-tuple-element.23), kind=kOutput, calls=%fused_computation.41 | convolution fusion | flops 408944640 | bytes 1050624 | tf_op jit(solution)/shard_map/pq,zqo->zpo/dot_general | solution.py:57
  78.6 34.1 %all-gather.2.cloned.1.call-done = bf16[1024,1024]{1,0:T(8,128)(2,1)} async-done(((bf16[1024,128]{1,0:T(8,128)(2,1)}), bf16[1024,1024]{1,0:T(8,128)(2,1)}) %all-gather.2.cloned.1.call-update) | async-done | bytes 2097168 | tf_op jit(solution)/shard_map/all_gather | solution.py:128
  112.8 2.1 %multiply_reduce_fusion = f32[1024]{0:T(1024)S(1)} fusion(bf16[1024,1024]{1,0:T(8,128)(2,1)} %all-gather.2.cloned.1.call-done), kind=kLoop, calls=%fused_computation | loop fusion | flops 3144704 | bytes 2101248 | tf_op jit(solution)/shard_map/reduce_sum | solution.py:134
  115.0 2.9 %copy.191 = bf16[1024,1024]{1,0:T(8,128)(2,1)S(1)} copy(bf16[1024,1024]{0,1:T(8,128)(2,1)} %bitcast.94) | data formatting | bytes 4194304 | tf_op jit(solution)/shard_map/dot_general | solution.py:91
  124.3 2.1 %collective-permute-done.10 = f32[2,2,2,2,2,17,256]{6,4,5,3,2,1,0:T(2,128)S(1)} collective-permute-done((f32[2,2,2,2,2,17,256]{6,4,5,3,2,1,0:T(2,128)}, f32[2,2,2,2,2,17,256]{6,4,5,3,2,1,0:T(2,128)S(1)}, u32[]{:S(2)}, u32[]{:S(2)}) %collective-permute-start.10) | collective-permute-done | bytes 557088 | tf_op jit(solution)/shard_map/ppermute | solution.py:110
  127.0 3.6 %collective-permute-start.11 = (f32[2,2,2,2,17,256]{5,3,4,2,1,0:T(2,128)S(1)}, f32[2,2,2,2,17,256]{5,3,4,2,1,0:T(2,128)S(1)}, u32[]{:S(2)}, u32[]{:S(2)}) collective-permute-start(f32[2,2,2,2,17,256]{5,3,4,2,1,0:T(2,128)S(1)} %select_bitcast_fusion.1), channel_id=1, source_target_pairs={{0,16},{8,24},{16,0},{24,8},{32,48},{40,56},{48,32},{56,40},{64,80... | collective-permute-start | bytes 835592 | tf_op jit(solution)/shard_map/ppermute | solution.py:110
  130.6 7.0 %collective-permute-done.11 = f32[2,2,2,2,17,256]{5,3,4,2,1,0:T(2,128)S(1)} collective-permute-done((f32[2,2,2,2,17,256]{5,3,4,2,1,0:T(2,128)S(1)}, f32[2,2,2,2,17,256]{5,3,4,2,1,0:T(2,128)S(1)}, u32[]{:S(2)}, u32[]{:S(2)}) %collective-permute-start.11) | collective-permute-done | bytes 278560 | tf_op jit(solution)/shard_map/ppermute | solution.py:110
  138.1 4.6 %collective-permute-start.12 = (f32[2,2,2,17,256]{4,2,3,1,0:T(2,128)S(1)}, f32[2,2,2,17,256]{4,2,3,1,0:T(2,128)S(1)}, u32[]{:S(2)}, u32[]{:S(2)}) collective-permute-start(f32[2,2,2,17,256]{4,2,3,1,0:T(2,128)S(1)} %bitcast.109), channel_id=1, source_target_pairs={{0,32},{8,40},{16,48},{24,56},{32,0},{40,8},{48,16},{56,24},{64,96... | collective-permute-start | bytes 417800 | tf_op jit(solution)/shard_map/ppermute | solution.py:110
  142.8 6.1 %collective-permute-done.12 = f32[2,2,2,17,256]{4,2,3,1,0:T(2,128)S(1)} collective-permute-done((f32[2,2,2,17,256]{4,2,3,1,0:T(2,128)S(1)}, f32[2,2,2,17,256]{4,2,3,1,0:T(2,128)S(1)}, u32[]{:S(2)}, u32[]{:S(2)}) %collective-permute-start.12) | collective-permute-done | bytes 139296 | tf_op jit(solution)/shard_map/ppermute | solution.py:110
  149.1 7.9 %collective-permute-start.13 = (f32[2,2,17,256]{3,1,2,0:T(2,128)S(1)}, f32[2,2,17,256]{3,1,2,0:T(2,128)S(1)}, u32[]{:S(2)}, u32[]{:S(2)}) collective-permute-start(f32[2,2,17,256]{3,1,2,0:T(2,128)S(1)} %bitcast.110), channel_id=1, source_target_pairs={{0,64},{8,72},{16,80},{24,88},{32,96},{40,104},{48,112},{56,120},{... | collective-permute-start | bytes 208904 | tf_op jit(solution)/shard_map/ppermute | solution.py:110
  157.0 2.3 %collective-permute-done.13 = f32[2,2,17,256]{3,1,2,0:T(2,128)S(1)} collective-permute-done((f32[2,2,17,256]{3,1,2,0:T(2,128)S(1)}, f32[2,2,17,256]{3,1,2,0:T(2,128)S(1)}, u32[]{:S(2)}, u32[]{:S(2)}) %collective-permute-start.13) | collective-permute-done | bytes 69664 | tf_op jit(solution)/shard_map/ppermute | solution.py:110
  159.5 4.0 %collective-permute-start.14 = (f32[2,17,256]{2,0,1:T(2,128)S(1)}, f32[2,17,256]{2,0,1:T(2,128)S(1)}, u32[]{:S(2)}, u32[]{:S(2)}) collective-permute-start(f32[2,17,256]{2,0,1:T(2,128)S(1)} %bitcast.111), channel_id=1, source_target_pairs={{0,128},{8,136},{16,144},{24,152},{32,160},{40,168},{48,176},{56,1... | collective-permute-start | bytes 104456 | tf_op jit(solution)/shard_map/ppermute | solution.py:110
  165.5 3.9 %collective-permute-start.15 = (f32[17,256]{1,0:T(8,128)S(1)}, f32[17,256]{1,0:T(8,128)S(1)}, u32[]{:S(2)}, u32[]{:S(2)}) collective-permute-start(f32[17,256]{1,0:T(8,128)S(1)} %bitcast.112), channel_id=1, source_target_pairs={{0,256},{8,264},{16,272},{24,280},{32,288},{40,296},{48,304},{56,3... | collective-permute-start | bytes 52232 | tf_op jit(solution)/shard_map/ppermute | solution.py:110
  169.4 3.3 %collective-permute-done.15 = f32[17,256]{1,0:T(8,128)S(1)} collective-permute-done((f32[17,256]{1,0:T(8,128)S(1)}, f32[17,256]{1,0:T(8,128)S(1)}, u32[]{:S(2)}, u32[]{:S(2)}) %collective-permute-start.15) | collective-permute-done | bytes 17440 | tf_op jit(solution)/shard_map/ppermute | solution.py:110
  (71 shorter events, 19.2 us)
Async XLA Ops:
  7.2 105.6 %all-gather.2.cloned.1.call-start = ((), (), s32[]{:S(2)}) async-start(), calls=%async_computation | async-start | bytes 2359296 | tf_op jit(solution)/shard_map/all_gather | solution.py:128
  8.3 15.8 %collective-permute-start = (bf16[4,16,16,128]{3,2,1,0:T(8,128)(2,1)S(1)}, bf16[4,16,16,128]{3,2,1,0:T(8,128)(2,1)S(1)}, u32[]{:S(2)}, u32[]{:S(2)}) collective-permute-start(bf16[4,16,16,128]{3,2,1,0:T(8,128)(2,1)S(1)} %convert_element_type.233), channel_id=1, source_target_pairs={{8,0},{16,8},{24,16},{32,24},{40,32},{48,40},{56,48},{64,56},{72,6... | collective-permute-start | bytes 786440 | tf_op jit(solution)/shard_map/ppermute | solution.py:22
  18.7 9.8 %collective-permute-start.1 = (bf16[4,16,16,128]{3,2,1,0:T(8,128)(2,1)S(1)}, bf16[4,16,16,128]{3,2,1,0:T(8,128)(2,1)S(1)}, u32[]{:S(2)}, u32[]{:S(2)}) collective-permute-start(bf16[4,16,16,128]{3,2,1,0:T(8,128)(2,1)S(1)} %convert_element_type.233), channel_id=1, source_target_pairs={{0,8},{8,16},{16,24},{24,32},{32,40},{40,48},{48,56},{56,64},{64,7... | collective-permute-start | bytes 786440 | tf_op jit(solution)/shard_map/ppermute | solution.py:21
  21.4 7.1 %copy-start = (f32[4,16,16,128]{3,2,1,0:T(8,128)S(1)}, f32[4,16,16,128]{3,2,1,0:T(8,128)}, u32[]{:S(2)}) copy-start(f32[4,16,16,128]{3,2,1,0:T(8,128)} %param.2) | copy-start | bytes 1572868
  21.4 7.2 %copy-start.2 = (f32[4,16,16]{2,1,0:T(8,128)S(1)}, f32[4,16,16]{2,1,0:T(8,128)}, u32[]{:S(2)}) copy-start(f32[4,16,16]{2,1,0:T(8,128)} %param.3) | copy-start | bytes 12292
  28.9 6.5 %collective-permute-start.2 = (bf16[4,16,16,128]{3,2,1,0:T(8,128)(2,1)S(1)}, bf16[4,16,16,128]{3,2,1,0:T(8,128)(2,1)S(1)}, u32[]{:S(2)}, u32[]{:S(2)}) collective-permute-start(bf16[4,16,16,128]{3,2,1,0:T(8,128)(2,1)S(1)} %get-tuple-element.9), channel_id=1, source_target_pairs={{8,0},{16,8},{24,16},{32,24},{40,32},{48,40},{56,48},{64,56},{72,6... | collective-permute-start | bytes 786440 | tf_op jit(solution)/shard_map/ppermute | solution.py:22
  30.8 9.8 %collective-permute-start.3 = (bf16[4,16,16,128]{3,2,1,0:T(8,128)(2,1)S(1)}, bf16[4,16,16,128]{3,2,1,0:T(8,128)(2,1)S(1)}, u32[]{:S(2)}, u32[]{:S(2)}) collective-permute-start(bf16[4,16,16,128]{3,2,1,0:T(8,128)(2,1)S(1)} %get-tuple-element.9), channel_id=1, source_target_pairs={{0,8},{8,16},{16,24},{24,32},{32,40},{40,48},{48,56},{56,64},{64,7... | collective-permute-start | bytes 786440 | tf_op jit(solution)/shard_map/ppermute | solution.py:21
  41.1 6.5 %collective-permute-start.4 = (bf16[4,16,16,128]{3,2,1,0:T(8,128)(2,1)S(1)}, bf16[4,16,16,128]{3,2,1,0:T(8,128)(2,1)S(1)}, u32[]{:S(2)}, u32[]{:S(2)}) collective-permute-start(bf16[4,16,16,128]{3,2,1,0:T(8,128)(2,1)S(1)} %get-tuple-element.7), channel_id=1, source_target_pairs={{8,0},{16,8},{24,16},{32,24},{40,32},{48,40},{56,48},{64,56},{72,6... | collective-permute-start | bytes 786440 | tf_op jit(solution)/shard_map/ppermute | solution.py:22
  43.1 9.8 %collective-permute-start.5 = (bf16[4,16,16,128]{3,2,1,0:T(8,128)(2,1)S(1)}, bf16[4,16,16,128]{3,2,1,0:T(8,128)(2,1)S(1)}, u32[]{:S(2)}, u32[]{:S(2)}) collective-permute-start(bf16[4,16,16,128]{3,2,1,0:T(8,128)(2,1)S(1)} %get-tuple-element.7), channel_id=1, source_target_pairs={{0,8},{8,16},{16,24},{24,32},{32,40},{40,48},{48,56},{56,64},{64,7... | collective-permute-start | bytes 786440 | tf_op jit(solution)/shard_map/ppermute | solution.py:21
  53.3 6.5 %collective-permute-start.6 = (bf16[4,16,16,128]{3,2,1,0:T(8,128)(2,1)S(1)}, bf16[4,16,16,128]{3,2,1,0:T(8,128)(2,1)S(1)}, u32[]{:S(2)}, u32[]{:S(2)}) collective-permute-start(bf16[4,16,16,128]{3,2,1,0:T(8,128)(2,1)S(1)} %get-tuple-element.5), channel_id=1, source_target_pairs={{8,0},{16,8},{24,16},{32,24},{40,32},{48,40},{56,48},{64,56},{72,6... | collective-permute-start | bytes 786440 | tf_op jit(solution)/shard_map/ppermute | solution.py:22
  55.2 9.8 %collective-permute-start.7 = (bf16[4,16,16,128]{3,2,1,0:T(8,128)(2,1)S(1)}, bf16[4,16,16,128]{3,2,1,0:T(8,128)(2,1)S(1)}, u32[]{:S(2)}, u32[]{:S(2)}) collective-permute-start(bf16[4,16,16,128]{3,2,1,0:T(8,128)(2,1)S(1)} %get-tuple-element.5), channel_id=1, source_target_pairs={{0,8},{8,16},{16,24},{24,32},{32,40},{40,48},{48,56},{56,64},{64,7... | collective-permute-start | bytes 786440 | tf_op jit(solution)/shard_map/ppermute | solution.py:21
  66.4 10.1 %collective-permute-start.9 = (bf16[4,16,16,128]{3,2,1,0:T(8,128)(2,1)}, bf16[4,16,16,128]{3,2,1,0:T(8,128)(2,1)S(1)}, u32[]{:S(2)}, u32[]{:S(2)}) collective-permute-start(bf16[4,16,16,128]{3,2,1,0:T(8,128)(2,1)} %convert_element_type.261), channel_id=1, source_target_pairs={{0,8},{8,16},{16,24},{24,32},{32,40},{40,48},{48,56},{56,64},{64,7... | collective-permute-start | bytes 786440 | tf_op jit(solution)/shard_map/ppermute | solution.py:21
  68.3 9.9 %collective-permute-start.8 = (bf16[4,16,16,128]{3,2,1,0:T(8,128)(2,1)}, bf16[4,16,16,128]{3,2,1,0:T(8,128)(2,1)S(1)}, u32[]{:S(2)}, u32[]{:S(2)}) collective-permute-start(bf16[4,16,16,128]{3,2,1,0:T(8,128)(2,1)} %convert_element_type.261), channel_id=1, source_target_pairs={{8,0},{16,8},{24,16},{32,24},{40,32},{48,40},{56,48},{64,56},{72,6... | collective-permute-start | bytes 786440 | tf_op jit(solution)/shard_map/ppermute | solution.py:22
  115.0 2.9 %copy-start.1 = (bf16[4,16,16,128]{3,2,1,0:T(8,128)(2,1)S(1)}, bf16[4,16,16,128]{3,2,1,0:T(8,128)(2,1)}, u32[]{:S(2)}) copy-start(bf16[4,16,16,128]{3,2,1,0:T(8,128)(2,1)} %convert_element_type.261) | copy-start | bytes 786436
  122.4 4.0 %collective-permute-start.10 = (f32[2,2,2,2,2,17,256]{6,4,5,3,2,1,0:T(2,128)}, f32[2,2,2,2,2,17,256]{6,4,5,3,2,1,0:T(2,128)S(1)}, u32[]{:S(2)}, u32[]{:S(2)}) collective-permute-start(f32[2,2,2,2,2,17,256]{6,4,5,3,2,1,0:T(2,128)} %copy.196), channel_id=1, source_target_pairs={{0,8},{8,0},{16,24},{24,16},{32,40},{40,32},{48,56},{56,48},{64,72... | collective-permute-start | bytes 1671176 | tf_op jit(solution)/shard_map/ppermute | solution.py:110
  127.0 10.6 %collective-permute-start.11 = (f32[2,2,2,2,17,256]{5,3,4,2,1,0:T(2,128)S(1)}, f32[2,2,2,2,17,256]{5,3,4,2,1,0:T(2,128)S(1)}, u32[]{:S(2)}, u32[]{:S(2)}) collective-permute-start(f32[2,2,2,2,17,256]{5,3,4,2,1,0:T(2,128)S(1)} %select_bitcast_fusion.1), channel_id=1, source_target_pairs={{0,16},{8,24},{16,0},{24,8},{32,48},{40,56},{48,32},{56,40},{64,80... | collective-permute-start | bytes 835592 | tf_op jit(solution)/shard_map/ppermute | solution.py:110
  138.1 10.7 %collective-permute-start.12 = (f32[2,2,2,17,256]{4,2,3,1,0:T(2,128)S(1)}, f32[2,2,2,17,256]{4,2,3,1,0:T(2,128)S(1)}, u32[]{:S(2)}, u32[]{:S(2)}) collective-permute-start(f32[2,2,2,17,256]{4,2,3,1,0:T(2,128)S(1)} %bitcast.109), channel_id=1, source_target_pairs={{0,32},{8,40},{16,48},{24,56},{32,0},{40,8},{48,16},{56,24},{64,96... | collective-permute-start | bytes 417800 | tf_op jit(solution)/shard_map/ppermute | solution.py:110
  149.1 10.2 %collective-permute-start.13 = (f32[2,2,17,256]{3,1,2,0:T(2,128)S(1)}, f32[2,2,17,256]{3,1,2,0:T(2,128)S(1)}, u32[]{:S(2)}, u32[]{:S(2)}) collective-permute-start(f32[2,2,17,256]{3,1,2,0:T(2,128)S(1)} %bitcast.110), channel_id=1, source_target_pairs={{0,64},{8,72},{16,80},{24,88},{32,96},{40,104},{48,112},{56,120},{... | collective-permute-start | bytes 208904 | tf_op jit(solution)/shard_map/ppermute | solution.py:110
  159.5 5.9 %collective-permute-start.14 = (f32[2,17,256]{2,0,1:T(2,128)S(1)}, f32[2,17,256]{2,0,1:T(2,128)S(1)}, u32[]{:S(2)}, u32[]{:S(2)}) collective-permute-start(f32[2,17,256]{2,0,1:T(2,128)S(1)} %bitcast.111), channel_id=1, source_target_pairs={{0,128},{8,136},{16,144},{24,152},{32,160},{40,168},{48,176},{56,1... | collective-permute-start | bytes 104456 | tf_op jit(solution)/shard_map/ppermute | solution.py:110
  165.5 7.2 %collective-permute-start.15 = (f32[17,256]{1,0:T(8,128)S(1)}, f32[17,256]{1,0:T(8,128)S(1)}, u32[]{:S(2)}, u32[]{:S(2)}) collective-permute-start(f32[17,256]{1,0:T(8,128)S(1)} %bitcast.112), channel_id=1, source_target_pairs={{0,256},{8,264},{16,272},{24,280},{32,288},{40,296},{48,304},{56,3... | collective-permute-start | bytes 52232 | tf_op jit(solution)/shard_map/ppermute | solution.py:110
Sparse Core Ops, SparseCore 0:
  66.4 46.3 all-gather.1
where the time goes:
time: 182 us; the launch traced here: 181 us
  waiting for transfers between devices  78.5 us (43%)
  starting transfers between devices  59.1 us (32%)
  between operations  14.6 us (8%)
  matrix products  11.8 us (6%)
  other arithmetic  11 us (6%)
  local copies, waits for them, and re-layouts  6.16 us (3%)
    all_gather x1, waiting for transfers between devices, on_device(): orbitals_all = lax.all_gather(rounded_orbitals, 'orb', axis=1, tiled=True)  34.1 us
    ppermute x6, starting transfers between devices, reduce_scatter_grid(): buf = keep + lax.ppermute(send, 'grid', pairs)  25.9 us
    ppermute x6, waiting for transfers between devices, reduce_scatter_grid(): buf = keep + lax.ppermute(send, 'grid', pairs)  22.7 us
    ppermute x5, starting transfers between devices, halo_layers(): after = lax.ppermute(initial, 'grid', down).astype(shard.dtype)  22.1 us
    ppermute x5, waiting for transfers between devices, halo_layers(): before = lax.ppermute(last, 'grid', up).astype(shard.dtype)  19.8 us
    ppermute x5, starting transfers between devices, halo_layers(): before = lax.ppermute(last, 'grid', up).astype(shard.dtype)  11 us
    dot_general x5, matrix products, apply_hamiltonian(): jnp.einsum('pq,zqo->zpo', plane, flat, precision=lax.Precision.HIGHEST, p...  10.4 us
  transfers between devices with their start and end apart: 17, of which 12 were waited for; matrix products, arithmetic and copies ran while one was open for 7% of the time, Pallas kernels for 0%

commit v1 on v0

--- a/solution.py
+++ b/solution.py
@@ -9,6 +9,38 @@
 CUT_EDGE = 1.5
 UPPER_EDGE = 10.0
 EPSILON = 1e-06
+
+
+def _handle_skins(unit, dim_no):
+    w1 = list(unit.shape[1:])
+    w1[dim_no] *= unit.shape[0]
+    all_rows = jnp.moveaxis(unit, 0, dim_no).reshape(w1)
+    return all_rows
+
+
+def plate_hold(chip_axis, dim_i, t0):
+    k_all = lax.psum(1, axis_name=chip_axis)
+    w2 = range(k_all)
+    even = map(lambda ix: (ix, (ix + 1) % k_all), w2)
+    made = list(even)
+    local_part, k_now = ([], [])
+    vals = [(hop_no, rr) for rr, hop_no in made]
+    for jj in tuple(range(k_all - 1)):
+        if jj % 2 == 0:
+            raw_out = lax.ppermute(
+                local_part[-1] if local_part else t0, axis_name=chip_axis, perm=made
+            )
+            local_part.append(raw_out)
+        else:
+            piece_next = lax.ppermute(k_now[-1] if k_now else t0, axis_name=chip_axis, perm=vals)
+            k_now.append(piece_next)
+    block_next = jnp.stack([*local_part[::-1], t0, *k_now])
+    extra = len(local_part)
+    val2 = lax.axis_index(chip_axis)
+    block_now = val2 - extra
+    block_next = block_next[(jnp.arange(k_all) - block_now) % k_all]
+    finding = _handle_skins(block_next, dim_i)
+    return finding
 
 
 def halo_layers(shard, width):
@@ -125,7 +157,7 @@
         .astype(jnp.bfloat16)
         .reshape(point_count, own_width)
     )
-    orbitals_all = lax.all_gather(rounded_orbitals, "orb", axis=1, tiled=True)
+    orbitals_all = plate_hold("orb", 1, rounded_orbitals)
     total_width = orbitals_all.shape[1]
     rows = total_width // grid_size
     hamiltonian_part = contract_points(orbitals_all, rounded_image)

time: 182 us -> 175 us (0.962)
  the two profiles are of different devices: /device:TPU:2 before, /device:TPU:30 now
where the time goes in v1:
time: 175 us; the launch traced here: 174 us
  starting transfers between devices  72.8 us (42%)
  waiting for transfers between devices  62.5 us (36%)
  local copies, waits for them, and re-layouts  15.2 us (9%)
  matrix products  13.6 us (8%)
  other arithmetic  8.68 us (5%)
    ppermute x6, waiting for transfers between devices, reduce_scatter_grid(): buf = keep + lax.ppermute(send, 'grid', pairs)  35.3 us
    ppermute x5, starting transfers between devices, halo_layers(): after = lax.ppermute(initial, 'grid', down).astype(shard.dtype)  22.2 us
    ppermute x4, starting transfers between devices, plate_hold(): lax.ppermute(local_part[-1] if local_part else t0, axis_name=chip_axis, p...  20.7 us
    ppermute x5, waiting for transfers between devices, halo_layers(): before = lax.ppermute(last, 'grid', up).astype(shard.dtype)  19.8 us
    ppermute x6, starting transfers between devices, reduce_scatter_grid(): buf = keep + lax.ppermute(send, 'grid', pairs)  13.1 us
    ppermute x5, starting transfers between devices, halo_layers(): before = lax.ppermute(last, 'grid', up).astype(shard.dtype)  11.1 us
    dot_general x5, matrix products, apply_hamiltonian(): jnp.einsum('pq,zqo->zpo', plane, flat, precision=lax.Precision.HIGHEST, p...  10.4 us
    unnamed x14, local copies, waits for them, and re-layouts  6.1 us
  transfers between devices with their start and end apart: 23, of which 13 were waited for; matrix products, arithmetic and copies ran while one was open for 11% of the time, Pallas kernels for 0%

profile of v1, /device:TPU:30, one launch (start us, length us, event | category | flops | bytes accessed | tf_op | source)
XLA Modules:
  0.0 174.0 jit_solution(16991870718522626047)
XLA Ops:
  1.7 10.7 %collective-permute-start = (bf16[4,16,16,128]{3,2,1,0:T(8,128)(2,1)S(1)}, bf16[4,16,16,128]{3,2,1,0:T(8,128)(2,1)S(1)}, u32[]{:S(2)}, u32[]{:S(2)}) collective-permute-start(bf16[4,16,16,128]{3,2,1,0:T(8,128)(2,1)S(1)} %convert_element_type.234), channel_id=1, source_target_pairs={{8,0},{16,8},{24,16},{32,24},{40,32},{48,40},{56,48},{64,56},{72,6... | collective-permute-start | bytes 786440 | tf_op jit(solution)/shard_map/ppermute | solution.py:54
  15.1 2.7 %fusion.102 = f32[256,4,128]{2,0,1:T(8,128)S(1)} fusion(f32[4,256,128]{2,1,0:T(8,128)} %bitcast.118, s32[256]{0:T(256)S(1)} %get-tuple-element.22, s32[256]{0:T(256)S(1)} %get-tuple-element.23), kind=kOutput, calls=%fused_computation.184 | convolution fusion | flops 408944640 | bytes 1050624 | tf_op jit(solution)/shard_map/pq,zqo->zpo/dot_general | solution.py:89
  17.9 4.3 %collective-permute-done.1 = bf16[4,16,16,128]{3,2,1,0:T(8,128)(2,1)S(1)} collective-permute-done((bf16[4,16,16,128]{3,2,1,0:T(8,128)(2,1)S(1)}, bf16[4,16,16,128]{3,2,1,0:T(8,128)(2,1)S(1)}, u32[]{:S(2)}, u32[]{:S(2)}) %collective-permute-start.1) | collective-permute-done | bytes 262176 | tf_op jit(solution)/shard_map/ppermute | solution.py:53
  22.6 1.9 %collective-permute-start.2 = (bf16[4,16,16,128]{3,2,1,0:T(8,128)(2,1)S(1)}, bf16[4,16,16,128]{3,2,1,0:T(8,128)(2,1)S(1)}, u32[]{:S(2)}, u32[]{:S(2)}) collective-permute-start(bf16[4,16,16,128]{3,2,1,0:T(8,128)(2,1)S(1)} %get-tuple-element.9), channel_id=1, source_target_pairs={{8,0},{16,8},{24,16},{32,24},{40,32},{48,40},{56,48},{64,56},{72,6... | collective-permute-start | bytes 786440 | tf_op jit(solution)/shard_map/ppermute | solution.py:54
  24.6 2.4 %collective-permute-start.3 = (bf16[4,16,16,128]{3,2,1,0:T(8,128)(2,1)S(1)}, bf16[4,16,16,128]{3,2,1,0:T(8,128)(2,1)S(1)}, u32[]{:S(2)}, u32[]{:S(2)}) collective-permute-start(bf16[4,16,16,128]{3,2,1,0:T(8,128)(2,1)S(1)} %get-tuple-element.9), channel_id=1, source_target_pairs={{0,8},{8,16},{16,24},{24,32},{32,40},{40,48},{48,56},{56,64},{64,7... | collective-permute-start | bytes 786440 | tf_op jit(solution)/shard_map/ppermute | solution.py:53
  27.0 1.9 %convolution_bitcast_fusion.3 = f32[4,256,128]{1,2,0:T(8,128)S(1)} fusion(f32[4,256,128]{2,1,0:T(8,128)S(1)} %bitcast.125, s32[256]{0:T(256)S(1)} %get-tuple-element.22, s32[256]{0:T(256)S(1)} %get-tuple-element.23), kind=kOutput, calls=%fused_computation.45 | convolution fusion | flops 408944640 | bytes 1050624 | tf_op jit(solution)/shard_map/pq,zqo->zpo/dot_general | solution.py:89
  29.2 5.1 %collective-permute-done.3 = bf16[4,16,16,128]{3,2,1,0:T(8,128)(2,1)S(1)} collective-permute-done((bf16[4,16,16,128]{3,2,1,0:T(8,128)(2,1)S(1)}, bf16[4,16,16,128]{3,2,1,0:T(8,128)(2,1)S(1)}, u32[]{:S(2)}, u32[]{:S(2)}) %collective-permute-start.3) | collective-permute-done | bytes 262176 | tf_op jit(solution)/shard_map/ppermute | solution.py:53
  36.8 2.4 %collective-permute-start.5 = (bf16[4,16,16,128]{3,2,1,0:T(8,128)(2,1)S(1)}, bf16[4,16,16,128]{3,2,1,0:T(8,128)(2,1)S(1)}, u32[]{:S(2)}, u32[]{:S(2)}) collective-permute-start(bf16[4,16,16,128]{3,2,1,0:T(8,128)(2,1)S(1)} %get-tuple-element.7), channel_id=1, source_target_pairs={{0,8},{8,16},{16,24},{24,32},{32,40},{40,48},{48,56},{56,64},{64,7... | collective-permute-start | bytes 786440 | tf_op jit(solution)/shard_map/ppermute | solution.py:53
  39.2 1.9 %convolution_bitcast_fusion.2 = f32[4,256,128]{1,2,0:T(8,128)S(1)} fusion(f32[4,256,128]{2,1,0:T(8,128)S(1)} %bitcast.119, s32[256]{0:T(256)S(1)} %get-tuple-element.22, s32[256]{0:T(256)S(1)} %get-tuple-element.23), kind=kOutput, calls=%fused_computation.44 | convolution fusion | flops 408944640 | bytes 1050624 | tf_op jit(solution)/shard_map/pq,zqo->zpo/dot_general | solution.py:89
  41.4 5.2 %collective-permute-done.5 = bf16[4,16,16,128]{3,2,1,0:T(8,128)(2,1)S(1)} collective-permute-done((bf16[4,16,16,128]{3,2,1,0:T(8,128)(2,1)S(1)}, bf16[4,16,16,128]{3,2,1,0:T(8,128)(2,1)S(1)}, u32[]{:S(2)}, u32[]{:S(2)}) %collective-permute-start.5) | collective-permute-done | bytes 262176 | tf_op jit(solution)/shard_map/ppermute | solution.py:53
  49.0 2.4 %collective-permute-start.7 = (bf16[4,16,16,128]{3,2,1,0:T(8,128)(2,1)S(1)}, bf16[4,16,16,128]{3,2,1,0:T(8,128)(2,1)S(1)}, u32[]{:S(2)}, u32[]{:S(2)}) collective-permute-start(bf16[4,16,16,128]{3,2,1,0:T(8,128)(2,1)S(1)} %get-tuple-element.5), channel_id=1, source_target_pairs={{0,8},{8,16},{16,24},{24,32},{32,40},{40,48},{48,56},{56,64},{64,7... | collective-permute-start | bytes 786440 | tf_op jit(solution)/shard_map/ppermute | solution.py:53
  51.4 1.9 %convolution_bitcast_fusion.1 = f32[4,256,128]{1,2,0:T(8,128)S(1)} fusion(f32[4,256,128]{2,1,0:T(8,128)S(1)} %bitcast.130, s32[256]{0:T(256)S(1)} %get-tuple-element.22, s32[256]{0:T(256)S(1)} %get-tuple-element.23), kind=kOutput, calls=%fused_computation.43 | convolution fusion | flops 408944640 | bytes 1050624 | tf_op jit(solution)/shard_map/pq,zqo->zpo/dot_general | solution.py:89
  53.6 5.2 %collective-permute-done.7 = bf16[4,16,16,128]{3,2,1,0:T(8,128)(2,1)S(1)} collective-permute-done((bf16[4,16,16,128]{3,2,1,0:T(8,128)(2,1)S(1)}, bf16[4,16,16,128]{3,2,1,0:T(8,128)(2,1)S(1)}, u32[]{:S(2)}, u32[]{:S(2)}) %collective-permute-start.7) | collective-permute-done | bytes 262176 | tf_op jit(solution)/shard_map/ppermute | solution.py:53
  59.3 4.7 %collective-permute-start.8 = (bf16[1024,128]{1,0:T(8,128)(2,1)S(1)}, bf16[1024,128]{1,0:T(8,128)(2,1)S(1)}, u32[]{:S(2)}, u32[]{:S(2)}) collective-permute-start(bf16[1024,128]{1,0:T(8,128)(2,1)S(1)} %bitcast.121), channel_id=1, source_target_pairs={{0,1},{1,2},{2,3},{3,4},{4,5},{5,6},{6,7},{7,0},{8,9},{9,10},{10,1... | collective-permute-start | bytes 786440 | tf_op jit(solution)/shard_map/ppermute | solution.py:30
  64.0 3.9 %collective-permute-done.8 = bf16[1024,128]{1,0:T(8,128)(2,1)S(1)} collective-permute-done((bf16[1024,128]{1,0:T(8,128)(2,1)S(1)}, bf16[1024,128]{1,0:T(8,128)(2,1)S(1)}, u32[]{:S(2)}, u32[]{:S(2)}) %collective-permute-start.8) | collective-permute-done | bytes 262176 | tf_op jit(solution)/shard_map/ppermute | solution.py:30
  67.9 5.6 %collective-permute-start.9 = (bf16[1024,128]{1,0:T(8,128)(2,1)S(1)}, bf16[1024,128]{1,0:T(8,128)(2,1)S(1)}, u32[]{:S(2)}, u32[]{:S(2)}) collective-permute-start(bf16[1024,128]{1,0:T(8,128)(2,1)S(1)} %collective-permute-done.8), channel_id=1, source_target_pairs={{0,1},{1,2},{2,3},{3,4},{4,5},{5,6},{6,7},{7,0},{8,9},{9,10},{10,1... | collective-permute-start | bytes 786440 | tf_op jit(solution)/shard_map/ppermute | solution.py:30
  77.4 5.8 %collective-permute-start.15 = (bf16[4,16,16,128]{3,2,1,0:T(8,128)(2,1)S(1)}, bf16[4,16,16,128]{3,2,1,0:T(8,128)(2,1)S(1)}, u32[]{:S(2)}, u32[]{:S(2)}) collective-permute-start(bf16[4,16,16,128]{3,2,1,0:T(8,128)(2,1)S(1)} %convert_element_type.262), channel_id=1, source_target_pairs={{8,0},{16,8},{24,16},{32,24},{40,32},{48,40},{56,48},{64,56},{72,6... | collective-permute-start | bytes 786440 | tf_op jit(solution)/shard_map/ppermute | solution.py:54
  83.2 5.3 %collective-permute-start.10 = (bf16[1024,128]{1,0:T(8,128)(2,1)S(1)}, bf16[1024,128]{1,0:T(8,128)(2,1)}, u32[]{:S(2)}, u32[]{:S(2)}) collective-permute-start(bf16[1024,128]{1,0:T(8,128)(2,1)S(1)} %collective-permute-done.9), channel_id=1, source_target_pairs={{0,1},{1,2},{2,3},{3,4},{4,5},{5,6},{6,7},{7,0},{8,9},{9,10},{10,1... | collective-permute-start | bytes 786440 | tf_op jit(solution)/shard_map/ppermute | solution.py:30
  88.5 1.9 %convolution_bitcast_fusion = f32[4,256,128]{1,2,0:T(8,128)S(1)} fusion(f32[4,256,128]{2,1,0:T(8,128)S(1)} %bitcast.117, s32[256]{0:T(256)S(1)} %get-tuple-element.22, s32[256]{0:T(256)S(1)} %get-tuple-element.23), kind=kOutput, calls=%fused_computation.42 | convolution fusion | flops 408944640 | bytes 1050624 | tf_op jit(solution)/shard_map/pq,zqo->zpo/dot_general | solution.py:89
  92.8 5.1 %collective-permute-start.11 = (bf16[1024,128]{1,0:T(8,128)(2,1)}, bf16[1024,128]{1,0:T(8,128)(2,1)S(1)}, u32[]{:S(2)}, u32[]{:S(2)}) collective-permute-start(bf16[1024,128]{1,0:T(8,128)(2,1)} %collective-permute-done.10), channel_id=1, source_target_pairs={{0,1},{1,2},{2,3},{3,4},{4,5},{5,6},{6,7},{7,0},{8,9},{9,10},{10,1... | collective-permute-start | bytes 786440 | tf_op jit(solution)/shard_map/ppermute | solution.py:30
  98.3 1.9 %collective-permute-done.13 = bf16[1024,128]{1,0:T(8,128)(2,1)S(1)} collective-permute-done((bf16[1024,128]{1,0:T(8,128)(2,1)S(1)}, bf16[1024,128]{1,0:T(8,128)(2,1)S(1)}, u32[]{:S(2)}, u32[]{:S(2)}) %collective-permute-start.13) | collective-permute-done | bytes 262176 | tf_op jit(solution)/shard_map/ppermute | solution.py:35
  110.4 2.5 %gather_fusion = bf16[8,1024,128]{2,1,0:T(8,128)(2,1)S(1)} fusion(bf16[8,1024,128]{2,1,0:T(8,128)(2,1)} %bitcast_dynamic-update-slice_fusion, s32[1024]{0:T(1024)S(1)} %pad_clamp_fusion), kind=kCustom, calls=%fused_computation | custom fusion | bytes 4194336 | tf_op jit(solution)/shard_map/gather | solution.py:41
  113.5 2.6 %copy.200 = bf16[1024,8,128]{0,2,1:T(8,128)(2,1)} copy(bf16[1024,8,128]{2,0,1:T(8,128)(2,1)S(1)} %bitcast.114) | data formatting | bytes 4194304 | tf_op jit(solution)/shard_map/transpose | solution.py:17
  116.1 2.4 %fusion.206 = f32[64,16,128]{2,1,0:T(8,128)S(1)} fusion(bf16[64,16,1024]{2,1,0:T(8,128)(2,1)} %bitcast.115, bf16[1024,128,1]{1,0,2:T(8,128)(2,1)S(1)} %bitcast.124), kind=kOutput, calls=%fused_computation.314 | convolution fusion | flops 268435456 | bytes 2883584 | tf_op jit(solution)/shard_map/dot_general | solution.py:123
  124.3 2.1 %collective-permute-done.17 = f32[2,2,2,2,2,17,256]{6,4,5,3,2,1,0:T(2,128)S(1)} collective-permute-done((f32[2,2,2,2,2,17,256]{6,4,5,3,2,1,0:T(2,128)}, f32[2,2,2,2,2,17,256]{6,4,5,3,2,1,0:T(2,128)S(1)}, u32[]{:S(2)}, u32[]{:S(2)}) %collective-permute-start.17) | collective-permute-done | bytes 557088 | tf_op jit(solution)/shard_map/ppermute | solution.py:142
  129.0 8.7 %collective-permute-done.18 = f32[2,2,2,2,17,256]{5,3,4,2,1,0:T(2,128)S(1)} collective-permute-done((f32[2,2,2,2,17,256]{5,3,4,2,1,0:T(2,128)S(1)}, f32[2,2,2,2,17,256]{5,3,4,2,1,0:T(2,128)S(1)}, u32[]{:S(2)}, u32[]{:S(2)}) %collective-permute-start.18) | collective-permute-done | bytes 278560 | tf_op jit(solution)/shard_map/ppermute | solution.py:142
  140.0 8.7 %collective-permute-done.19 = f32[2,2,2,17,256]{4,2,3,1,0:T(2,128)S(1)} collective-permute-done((f32[2,2,2,17,256]{4,2,3,1,0:T(2,128)S(1)}, f32[2,2,2,17,256]{4,2,3,1,0:T(2,128)S(1)}, u32[]{:S(2)}, u32[]{:S(2)}) %collective-permute-start.19) | collective-permute-done | bytes 139296 | tf_op jit(solution)/shard_map/ppermute | solution.py:142
  151.0 8.2 %collective-permute-done.20 = f32[2,2,17,256]{3,1,2,0:T(2,128)S(1)} collective-permute-done((f32[2,2,17,256]{3,1,2,0:T(2,128)S(1)}, f32[2,2,17,256]{3,1,2,0:T(2,128)S(1)}, u32[]{:S(2)}, u32[]{:S(2)}) %collective-permute-start.20) | collective-permute-done | bytes 69664 | tf_op jit(solution)/shard_map/ppermute | solution.py:142
  159.3 2.4 %collective-permute-start.21 = (f32[2,17,256]{2,0,1:T(2,128)S(1)}, f32[2,17,256]{2,0,1:T(2,128)S(1)}, u32[]{:S(2)}, u32[]{:S(2)}) collective-permute-start(f32[2,17,256]{2,0,1:T(2,128)S(1)} %bitcast.135), channel_id=1, source_target_pairs={{0,128},{8,136},{16,144},{24,152},{32,160},{40,168},{48,176},{56,1... | collective-permute-start | bytes 104456 | tf_op jit(solution)/shard_map/ppermute | solution.py:142
  161.7 3.4 %collective-permute-done.21 = f32[2,17,256]{2,0,1:T(2,128)S(1)} collective-permute-done((f32[2,17,256]{2,0,1:T(2,128)S(1)}, f32[2,17,256]{2,0,1:T(2,128)S(1)}, u32[]{:S(2)}, u32[]{:S(2)}) %collective-permute-start.21) | collective-permute-done | bytes 34848 | tf_op jit(solution)/shard_map/ppermute | solution.py:142
  165.2 3.0 %collective-permute-start.22 = (f32[17,256]{1,0:T(8,128)S(1)}, f32[17,256]{1,0:T(8,128)S(1)}, u32[]{:S(2)}, u32[]{:S(2)}) collective-permute-start(f32[17,256]{1,0:T(8,128)S(1)} %bitcast.136), channel_id=1, source_target_pairs={{0,256},{8,264},{16,272},{24,280},{32,288},{40,296},{48,304},{56,3... | collective-permute-start | bytes 52232 | tf_op jit(solution)/shard_map/ppermute | solution.py:142
  168.2 4.2 %collective-permute-done.22 = f32[17,256]{1,0:T(8,128)S(1)} collective-permute-done((f32[17,256]{1,0:T(8,128)S(1)}, f32[17,256]{1,0:T(8,128)S(1)}, u32[]{:S(2)}, u32[]{:S(2)}) %collective-permute-start.22) | collective-permute-done | bytes 17440 | tf_op jit(solution)/shard_map/ppermute | solution.py:142
  (93 shorter events, 42.0 us)
Async XLA Ops:
  1.7 16.1 %collective-permute-start = (bf16[4,16,16,128]{3,2,1,0:T(8,128)(2,1)S(1)}, bf16[4,16,16,128]{3,2,1,0:T(8,128)(2,1)S(1)}, u32[]{:S(2)}, u32[]{:S(2)}) collective-permute-start(bf16[4,16,16,128]{3,2,1,0:T(8,128)(2,1)S(1)} %convert_element_type.234), channel_id=1, source_target_pairs={{8,0},{16,8},{24,16},{32,24},{40,32},{48,40},{56,48},{64,56},{72,6... | collective-permute-start | bytes 786440 | tf_op jit(solution)/shard_map/ppermute | solution.py:54
  12.4 9.8 %collective-permute-start.1 = (bf16[4,16,16,128]{3,2,1,0:T(8,128)(2,1)S(1)}, bf16[4,16,16,128]{3,2,1,0:T(8,128)(2,1)S(1)}, u32[]{:S(2)}, u32[]{:S(2)}) collective-permute-start(bf16[4,16,16,128]{3,2,1,0:T(8,128)(2,1)S(1)} %convert_element_type.234), channel_id=1, source_target_pairs={{0,8},{8,16},{16,24},{24,32},{32,40},{40,48},{48,56},{56,64},{64,7... | collective-permute-start | bytes 786440 | tf_op jit(solution)/shard_map/ppermute | solution.py:53
  15.1 7.1 %copy-start.1 = (f32[4,16,16,128]{3,2,1,0:T(8,128)S(1)}, f32[4,16,16,128]{3,2,1,0:T(8,128)}, u32[]{:S(2)}) copy-start(f32[4,16,16,128]{3,2,1,0:T(8,128)} %param.2) | copy-start | bytes 1572868
  15.1 7.2 %copy-start.2 = (f32[4,16,16]{2,1,0:T(8,128)S(1)}, f32[4,16,16]{2,1,0:T(8,128)}, u32[]{:S(2)}) copy-start(f32[4,16,16]{2,1,0:T(8,128)} %param.3) | copy-start | bytes 12292
  22.6 6.5 %collective-permute-start.2 = (bf16[4,16,16,128]{3,2,1,0:T(8,128)(2,1)S(1)}, bf16[4,16,16,128]{3,2,1,0:T(8,128)(2,1)S(1)}, u32[]{:S(2)}, u32[]{:S(2)}) collective-permute-start(bf16[4,16,16,128]{3,2,1,0:T(8,128)(2,1)S(1)} %get-tuple-element.9), channel_id=1, source_target_pairs={{8,0},{16,8},{24,16},{32,24},{40,32},{48,40},{56,48},{64,56},{72,6... | collective-permute-start | bytes 786440 | tf_op jit(solution)/shard_map/ppermute | solution.py:54
  24.6 9.8 %collective-permute-start.3 = (bf16[4,16,16,128]{3,2,1,0:T(8,128)(2,1)S(1)}, bf16[4,16,16,128]{3,2,1,0:T(8,128)(2,1)S(1)}, u32[]{:S(2)}, u32[]{:S(2)}) collective-permute-start(bf16[4,16,16,128]{3,2,1,0:T(8,128)(2,1)S(1)} %get-tuple-element.9), channel_id=1, source_target_pairs={{0,8},{8,16},{16,24},{24,32},{32,40},{40,48},{48,56},{56,64},{64,7... | collective-permute-start | bytes 786440 | tf_op jit(solution)/shard_map/ppermute | solution.py:53
  34.8 6.5 %collective-permute-start.4 = (bf16[4,16,16,128]{3,2,1,0:T(8,128)(2,1)S(1)}, bf16[4,16,16,128]{3,2,1,0:T(8,128)(2,1)S(1)}, u32[]{:S(2)}, u32[]{:S(2)}) collective-permute-start(bf16[4,16,16,128]{3,2,1,0:T(8,128)(2,1)S(1)} %get-tuple-element.7), channel_id=1, source_target_pairs={{8,0},{16,8},{24,16},{32,24},{40,32},{48,40},{56,48},{64,56},{72,6... | collective-permute-start | bytes 786440 | tf_op jit(solution)/shard_map/ppermute | solution.py:54
  36.8 9.8 %collective-permute-start.5 = (bf16[4,16,16,128]{3,2,1,0:T(8,128)(2,1)S(1)}, bf16[4,16,16,128]{3,2,1,0:T(8,128)(2,1)S(1)}, u32[]{:S(2)}, u32[]{:S(2)}) collective-permute-start(bf16[4,16,16,128]{3,2,1,0:T(8,128)(2,1)S(1)} %get-tuple-element.7), channel_id=1, source_target_pairs={{0,8},{8,16},{16,24},{24,32},{32,40},{40,48},{48,56},{56,64},{64,7... | collective-permute-start | bytes 786440 | tf_op jit(solution)/shard_map/ppermute | solution.py:53
  47.0 6.5 %collective-permute-start.6 = (bf16[4,16,16,128]{3,2,1,0:T(8,128)(2,1)S(1)}, bf16[4,16,16,128]{3,2,1,0:T(8,128)(2,1)S(1)}, u32[]{:S(2)}, u32[]{:S(2)}) collective-permute-start(bf16[4,16,16,128]{3,2,1,0:T(8,128)(2,1)S(1)} %get-tuple-element.5), channel_id=1, source_target_pairs={{8,0},{16,8},{24,16},{32,24},{40,32},{48,40},{56,48},{64,56},{72,6... | collective-permute-start | bytes 786440 | tf_op jit(solution)/shard_map/ppermute | solution.py:54
  49.0 9.8 %collective-permute-start.7 = (bf16[4,16,16,128]{3,2,1,0:T(8,128)(2,1)S(1)}, bf16[4,16,16,128]{3,2,1,0:T(8,128)(2,1)S(1)}, u32[]{:S(2)}, u32[]{:S(2)}) collective-permute-start(bf16[4,16,16,128]{3,2,1,0:T(8,128)(2,1)S(1)} %get-tuple-element.5), channel_id=1, source_target_pairs={{0,8},{8,16},{16,24},{24,32},{32,40},{40,48},{48,56},{56,64},{64,7... | collective-permute-start | bytes 786440 | tf_op jit(solution)/shard_map/ppermute | solution.py:53
  59.3 8.6 %collective-permute-start.8 = (bf16[1024,128]{1,0:T(8,128)(2,1)S(1)}, bf16[1024,128]{1,0:T(8,128)(2,1)S(1)}, u32[]{:S(2)}, u32[]{:S(2)}) collective-permute-start(bf16[1024,128]{1,0:T(8,128)(2,1)S(1)} %bitcast.121), channel_id=1, source_target_pairs={{0,1},{1,2},{2,3},{3,4},{4,5},{5,6},{6,7},{7,0},{8,9},{9,10},{10,1... | collective-permute-start | bytes 786440 | tf_op jit(solution)/shard_map/ppermute | solution.py:30
  67.9 15.3 %collective-permute-start.9 = (bf16[1024,128]{1,0:T(8,128)(2,1)S(1)}, bf16[1024,128]{1,0:T(8,128)(2,1)S(1)}, u32[]{:S(2)}, u32[]{:S(2)}) collective-permute-start(bf16[1024,128]{1,0:T(8,128)(2,1)S(1)} %collective-permute-done.8), channel_id=1, source_target_pairs={{0,1},{1,2},{2,3},{3,4},{4,5},{5,6},{6,7},{7,0},{8,9},{9,10},{10,1... | collective-permute-start | bytes 786440 | tf_op jit(solution)/shard_map/ppermute | solution.py:30
  73.6 17.2 %collective-permute-start.12 = (bf16[1024,128]{1,0:T(8,128)(2,1)S(1)}, bf16[1024,128]{1,0:T(8,128)(2,1)S(1)}, u32[]{:S(2)}, u32[]{:S(2)}) collective-permute-start(bf16[1024,128]{1,0:T(8,128)(2,1)S(1)} %bitcast.122), channel_id=1, source_target_pairs={{1,0},{2,1},{3,2},{4,3},{5,4},{6,5},{7,6},{0,7},{9,8},{10,9},{11,1... | collective-permute-start | bytes 786440 | tf_op jit(solution)/shard_map/ppermute | solution.py:35
  75.5 17.2 %collective-permute-start.16 = (bf16[4,16,16,128]{3,2,1,0:T(8,128)(2,1)S(1)}, bf16[4,16,16,128]{3,2,1,0:T(8,128)(2,1)S(1)}, u32[]{:S(2)}, u32[]{:S(2)}) collective-permute-start(bf16[4,16,16,128]{3,2,1,0:T(8,128)(2,1)S(1)} %convert_element_type.262), channel_id=1, source_target_pairs={{0,8},{8,16},{16,24},{24,32},{32,40},{40,48},{48,56},{56,64},{64,7... | collective-permute-start | bytes 786440 | tf_op jit(solution)/shard_map/ppermute | solution.py:53
  77.4 15.3 %collective-permute-start.15 = (bf16[4,16,16,128]{3,2,1,0:T(8,128)(2,1)S(1)}, bf16[4,16,16,128]{3,2,1,0:T(8,128)(2,1)S(1)}, u32[]{:S(2)}, u32[]{:S(2)}) collective-permute-start(bf16[4,16,16,128]{3,2,1,0:T(8,128)(2,1)S(1)} %convert_element_type.262), channel_id=1, source_target_pairs={{8,0},{16,8},{24,16},{32,24},{40,32},{48,40},{56,48},{64,56},{72,6... | collective-permute-start | bytes 786440 | tf_op jit(solution)/shard_map/ppermute | solution.py:54
  83.2 9.6 %collective-permute-start.10 = (bf16[1024,128]{1,0:T(8,128)(2,1)S(1)}, bf16[1024,128]{1,0:T(8,128)(2,1)}, u32[]{:S(2)}, u32[]{:S(2)}) collective-permute-start(bf16[1024,128]{1,0:T(8,128)(2,1)S(1)} %collective-permute-done.9), channel_id=1, source_target_pairs={{0,1},{1,2},{2,3},{3,4},{4,5},{5,6},{6,7},{7,0},{8,9},{9,10},{10,1... | collective-permute-start | bytes 786440 | tf_op jit(solution)/shard_map/ppermute | solution.py:30
  90.7 9.5 %collective-permute-start.13 = (bf16[1024,128]{1,0:T(8,128)(2,1)S(1)}, bf16[1024,128]{1,0:T(8,128)(2,1)S(1)}, u32[]{:S(2)}, u32[]{:S(2)}) collective-permute-start(bf16[1024,128]{1,0:T(8,128)(2,1)S(1)} %collective-permute-done.12), channel_id=1, source_target_pairs={{1,0},{2,1},{3,2},{4,3},{5,4},{6,5},{7,6},{0,7},{9,8},{10,9},{11,1... | collective-permute-start | bytes 786440 | tf_op jit(solution)/shard_map/ppermute | solution.py:35
  92.8 9.3 %collective-permute-start.11 = (bf16[1024,128]{1,0:T(8,128)(2,1)}, bf16[1024,128]{1,0:T(8,128)(2,1)S(1)}, u32[]{:S(2)}, u32[]{:S(2)}) collective-permute-start(bf16[1024,128]{1,0:T(8,128)(2,1)} %collective-permute-done.10), channel_id=1, source_target_pairs={{0,1},{1,2},{2,3},{3,4},{4,5},{5,6},{6,7},{7,0},{8,9},{9,10},{10,1... | collective-permute-start | bytes 786440 | tf_op jit(solution)/shard_map/ppermute | solution.py:30
  100.2 9.5 %collective-permute-start.14 = (bf16[1024,128]{1,0:T(8,128)(2,1)S(1)}, bf16[1024,128]{1,0:T(8,128)(2,1)S(1)}, u32[]{:S(2)}, u32[]{:S(2)}) collective-permute-start(bf16[1024,128]{1,0:T(8,128)(2,1)S(1)} %collective-permute-done.13), channel_id=1, source_target_pairs={{1,0},{2,1},{3,2},{4,3},{5,4},{6,5},{7,6},{0,7},{9,8},{10,9},{11,1... | collective-permute-start | bytes 786440 | tf_op jit(solution)/shard_map/ppermute | solution.py:35
  116.1 2.4 %copy-start = (bf16[1024,8,128]{0,2,1:T(8,128)(2,1)S(1)}, bf16[1024,8,128]{0,2,1:T(8,128)(2,1)}, u32[]{:S(2)}) copy-start(bf16[1024,8,128]{0,2,1:T(8,128)(2,1)} %copy.200) | copy-start | bytes 6291460
  122.3 4.0 %collective-permute-start.17 = (f32[2,2,2,2,2,17,256]{6,4,5,3,2,1,0:T(2,128)}, f32[2,2,2,2,2,17,256]{6,4,5,3,2,1,0:T(2,128)S(1)}, u32[]{:S(2)}, u32[]{:S(2)}) collective-permute-start(f32[2,2,2,2,2,17,256]{6,4,5,3,2,1,0:T(2,128)} %copy.205), channel_id=1, source_target_pairs={{0,8},{8,0},{16,24},{24,16},{32,40},{40,32},{48,56},{56,48},{64,72... | collective-permute-start | bytes 1671176 | tf_op jit(solution)/shard_map/ppermute | solution.py:142
  127.0 10.6 %collective-permute-start.18 = (f32[2,2,2,2,17,256]{5,3,4,2,1,0:T(2,128)S(1)}, f32[2,2,2,2,17,256]{5,3,4,2,1,0:T(2,128)S(1)}, u32[]{:S(2)}, u32[]{:S(2)}) collective-permute-start(f32[2,2,2,2,17,256]{5,3,4,2,1,0:T(2,128)S(1)} %select_bitcast_fusion.1), channel_id=1, source_target_pairs={{0,16},{8,24},{16,0},{24,8},{32,48},{40,56},{48,32},{56,40},{64,80... | collective-permute-start | bytes 835592 | tf_op jit(solution)/shard_map/ppermute | solution.py:142
  138.1 10.7 %collective-permute-start.19 = (f32[2,2,2,17,256]{4,2,3,1,0:T(2,128)S(1)}, f32[2,2,2,17,256]{4,2,3,1,0:T(2,128)S(1)}, u32[]{:S(2)}, u32[]{:S(2)}) collective-permute-start(f32[2,2,2,17,256]{4,2,3,1,0:T(2,128)S(1)} %bitcast.133), channel_id=1, source_target_pairs={{0,32},{8,40},{16,48},{24,56},{32,0},{40,8},{48,16},{56,24},{64,96... | collective-permute-start | bytes 417800 | tf_op jit(solution)/shard_map/ppermute | solution.py:142
  149.0 10.1 %collective-permute-start.20 = (f32[2,2,17,256]{3,1,2,0:T(2,128)S(1)}, f32[2,2,17,256]{3,1,2,0:T(2,128)S(1)}, u32[]{:S(2)}, u32[]{:S(2)}) collective-permute-start(f32[2,2,17,256]{3,1,2,0:T(2,128)S(1)} %bitcast.134), channel_id=1, source_target_pairs={{0,64},{8,72},{16,80},{24,88},{32,96},{40,104},{48,112},{56,120},{... | collective-permute-start | bytes 208904 | tf_op jit(solution)/shard_map/ppermute | solution.py:142
  159.3 5.8 %collective-permute-start.21 = (f32[2,17,256]{2,0,1:T(2,128)S(1)}, f32[2,17,256]{2,0,1:T(2,128)S(1)}, u32[]{:S(2)}, u32[]{:S(2)}) collective-permute-start(f32[2,17,256]{2,0,1:T(2,128)S(1)} %bitcast.135), channel_id=1, source_target_pairs={{0,128},{8,136},{16,144},{24,152},{32,160},{40,168},{48,176},{56,1... | collective-permute-start | bytes 104456 | tf_op jit(solution)/shard_map/ppermute | solution.py:142
  165.2 7.2 %collective-permute-start.22 = (f32[17,256]{1,0:T(8,128)S(1)}, f32[17,256]{1,0:T(8,128)S(1)}, u32[]{:S(2)}, u32[]{:S(2)}) collective-permute-start(f32[17,256]{1,0:T(8,128)S(1)} %bitcast.136), channel_id=1, source_target_pairs={{0,256},{8,264},{16,272},{24,280},{32,288},{40,296},{48,304},{56,3... | collective-permute-start | bytes 52232 | tf_op jit(solution)/shard_map/ppermute | solution.py:142
